TPU v7x, 256 devices: a whole 4x4x8 slice. The times are simulated.
256 devices in a mesh: ctx: 32 (over y, x, core), exp: 8 (over z).
Axes of the slice: x: 4, y: 4, z: 8, core: 2. Of those that a mesh axis runs over, the one named last changes fastest.
Arguments:
- ssm_input: bfloat16 [4096, 4096], P('ctx', 'exp'), may hold values from -6 to 6
- gate_input: bfloat16 [4096, 4096], P('ctx', 'exp'), may hold values from -6 to 6
- key_proj: bfloat16 [4096, 128], P('ctx'), may hold values from -4 to 4
- query_proj: bfloat16 [4096, 128], P('ctx'), may hold values from -4 to 4
- step_size: float32 [4096, 64], P('ctx', 'exp'), may hold values from 0 to 1, as said below
- decay_rate: float32 [64], P('exp'), may hold values from 0.5 to 1.5
- head_gain: float32 [4096], P('exp'), may hold values from 0.5 to 1.5
- residual: bfloat16 [4096, 4096], P('ctx', 'exp'), may hold values from -33 to 33
- ffn_gain: float32 [4096], replicated, may hold values from 0.5 to 1.5
- gate_weight: bfloat16 [8, 4096, 12288], P('exp', None, 'ctx'), may hold values from -0.09375 to 0.09375
- up_weight: bfloat16 [8, 4096, 12288], P('exp', None, 'ctx'), may hold values from -0.09375 to 0.09375
- down_weight: bfloat16 [8, 12288, 4096], P('exp', 'ctx'), may hold values from -0.0546875 to 0.0546875
- expert_ids: int32 [4096, 2], P('ctx'), may hold values from 0 to 7, all different within a row; in each aligned block of 128 rows (0 to 127, 128 to 255, ...) at most 48 rows name the same one
- route_weight: float32 [4096, 2], P('ctx'), may hold values from 0.5 to 2
Outputs:
- block_out: bfloat16 [4096, 4096], P('ctx', 'exp')
- expert_out: bfloat16 [4096, 4096], P('ctx', 'exp')
Inputs may be any that keep to these rules, and one draw needn't show every extreme that they name: `step_size`: step sizes are positive. `expert_ids`: the two experts of a token differ. In each aligned block of 128 rows (the tokens of one shard) no expert is named by more than 48 rows, and in some block one expert is named by exactly 48 rows.
All inputs are finite; a program needn't handle non-finite values.
Results may differ from a plain program's by a relative error of at most 0.022.
Values may be sent and summed in bfloat16 or wider, within the bound.
No kernel may reach another device: no remote copies, remote signals or barrier semaphores. Data moves between devices by JAX's collectives and lax.ppermute only.
A program may use at most 128 MiB of HBM per device.

v0:
```python
import jax
import jax.numpy as jnp
from jax import lax
from jax.sharding import Mesh, PartitionSpec as P

precise = lax.Precision.HIGHEST
CTX = ("chip", "core")


def local_block(ssm_piece, key_piece, query_piece, step_piece, decay_rate, head_count):
    row_count = ssm_piece.shape[0]
    head_width = ssm_piece.shape[1] // head_count
    values = ssm_piece.astype(jnp.float32).reshape(row_count, head_count, head_width)
    key_vals = key_piece.astype(jnp.float32)
    queries = query_piece.astype(jnp.float32)
    log_steps = -step_piece * decay_rate[None, :]
    running = jnp.cumsum(log_steps, axis=0)
    scores = jnp.dot(queries, key_vals.T, precision=precise)
    causal = (jnp.arange(row_count)[:, None] >= jnp.arange(row_count)[None, :])[:, :, None]
    spacing = running[:, None, :] - running[None, :, :]
    decays = jnp.where(causal, jnp.exp(jnp.where(causal, spacing, 0.0)), 0.0)
    within = jnp.einsum("tsh,ts,shp->thp", decays, scores, values, precision=precise)
    overall = running[-1]
    fading = jnp.exp(overall[None, :] - running)
    states = jnp.einsum("sh,shp,sn->hpn", fading, values, key_vals, precision=precise)
    return (within, running, overall, states)


def route_tables(expert_ids, route_weight, experts, capacity):
    matched = expert_ids[None, :, :] == experts[:, None, None]
    member = jnp.any(matched, axis=2).astype(jnp.int32)
    gate_sum = jnp.sum(jnp.where(matched, route_weight[None, :, :], 0.0), axis=2)
    slot_index = jnp.cumsum(member, axis=1) - 1
    positions = jnp.arange(capacity, dtype=jnp.int32)
    routing = (
        (slot_index[:, None, :] == positions[None, :, None]) & (member[:, None, :] > 0)
    ).astype(jnp.float32)
    return (routing, gate_sum)


def carried_state(overall, states):
    head_count, head_width, nstate = states.shape
    rows = head_count * head_width
    high = overall.astype(jnp.bfloat16)
    low = (overall - high.astype(jnp.float32)).astype(jnp.bfloat16)
    extra = jnp.zeros((8, nstate), jnp.bfloat16)
    extra = extra.at[0, :head_count].set(high).at[1, :head_count].set(low)
    packed = jnp.concatenate([states.astype(jnp.bfloat16).reshape(rows, nstate), extra], axis=0)
    everything = lax.all_gather(packed, CTX)
    shards = everything.shape[0]
    me = lax.axis_index(CTX)
    decay_all = everything[:, rows, :head_count].astype(jnp.float32) + everything[
        :, rows + 1, :head_count
    ].astype(jnp.float32)
    shard_of = jnp.arange(shards, dtype=jnp.int32)
    between = (shard_of[:, None] < shard_of[None, :]) & (shard_of[None, :] < me)
    spans = jnp.sum(jnp.where(between[:, :, None], decay_all[None, :, :], 0.0), axis=1)
    weight = jnp.where((shard_of < me)[:, None], jnp.exp(spans), 0.0)
    gathered = (
        everything[:, :rows, :].astype(jnp.float32).reshape(shards, head_count, head_width, nstate)
    )
    return jnp.sum(weight[:, :, None, None] * gathered, axis=0)


def on_device(
    ssm_input,
    gate_input,
    key_proj,
    query_proj,
    step_size,
    decay_rate,
    head_gain,
    residual,
    ffn_gain,
    gate_weight,
    up_weight,
    down_weight,
    expert_ids,
    route_weight,
):
    head_count = step_size.shape[1]
    row_count, channels = ssm_input.shape
    head_width = channels // head_count
    within, running, overall, states = local_block(
        ssm_input, key_proj, query_proj, step_size, decay_rate, head_count
    )
    before = carried_state(overall, states)
    carried = jnp.einsum(
        "th,hpn,tn->thp",
        jnp.exp(running),
        before,
        query_proj.astype(jnp.float32),
        precision=precise,
    )
    mixer_out = within + carried
    gated_out = mixer_out * jax.nn.silu(gate_input.astype(jnp.float32)).reshape(
        row_count, head_count, head_width
    )
    inv_rms = lax.rsqrt(jnp.mean(gated_out * gated_out, axis=2, keepdims=True) + 1e-05)
    normed = (gated_out * inv_rms).reshape(row_count, channels) * head_gain[None, :]
    block_out = (residual.astype(jnp.float32) + normed).astype(jnp.bfloat16)
    exp_count = lax.axis_size("exp")
    capacity = 3 * row_count // exp_count
    tables, gate_sum = route_tables(
        expert_ids, route_weight, jnp.arange(exp_count, dtype=jnp.int32), capacity
    )
    picked = jnp.einsum(
        "ekt,td->ekd", tables.astype(jnp.bfloat16), block_out, preferred_element_type=jnp.float32
    ).astype(jnp.bfloat16)
    arrived = lax.all_to_all(picked, "exp", 0, 0)
    own_rows = jnp.transpose(arrived, (1, 0, 2)).reshape(capacity, exp_count * channels)
    widened = own_rows.astype(jnp.float32)
    chosen = (
        widened
        * lax.rsqrt(jnp.mean(widened * widened, axis=1, keepdims=True) + 1e-06)
        * ffn_gain[None, :]
    ).astype(jnp.bfloat16)
    gate_here = gate_weight[0]
    up_here = up_weight[0]
    down_here = down_weight[0]
    swap = [(0, 1), (1, 0)]
    gate_other = lax.ppermute(gate_here, "core", swap)
    up_other = lax.ppermute(up_here, "core", swap)
    down_other = lax.ppermute(down_here, "core", swap)
    token_piece = lax.all_gather(chosen, "chip", axis=0, tiled=True)
    gate_both = jnp.concatenate([gate_here, gate_other], axis=1)
    up_both = jnp.concatenate([up_here, up_other], axis=1)
    down_both = jnp.concatenate([down_here, down_other], axis=0)
    gate_proj = jnp.dot(token_piece, gate_both, preferred_element_type=jnp.float32)
    up_proj = jnp.dot(token_piece, up_both, preferred_element_type=jnp.float32)
    hidden = (jax.nn.silu(gate_proj) * up_proj).astype(jnp.bfloat16)
    pair_sum = jnp.dot(hidden, down_both, preferred_element_type=jnp.float32).astype(jnp.bfloat16)
    summed = lax.psum_scatter(pair_sum, "chip", scatter_dimension=0, tiled=True)
    outgoing = jnp.transpose(summed.reshape(capacity, exp_count, channels), (1, 0, 2))
    returned = lax.all_to_all(outgoing, "exp", 0, 0)
    weights = tables * gate_sum[:, None, :]
    expert_out = jnp.einsum(
        "ekt,ekd->td", weights, returned.astype(jnp.float32), precision=precise
    ).astype(jnp.bfloat16)
    return (block_out, expert_out)


def solution(mesh):
    ctx_size, exp_size = mesh.devices.shape
    split = Mesh(mesh.devices.reshape(ctx_size // 2, 2, exp_size), ("chip", "core", "exp"))
    placed = (
        P(CTX, "exp"),
        P(CTX, "exp"),
        P(CTX, None),
        P(CTX, None),
        P(CTX, "exp"),
        P("exp"),
        P("exp"),
        P(CTX, "exp"),
        P(),
        P("exp", None, CTX),
        P("exp", None, CTX),
        P("exp", CTX, None),
        P(CTX, None),
        P(CTX, None),
    )
    return jax.shard_map(
        on_device,
        mesh=split,
        in_specs=placed,
        out_specs=(P(CTX, "exp"), P(CTX, "exp")),
        check_vma=False,
    )
```

profile of v0, /device:TPU:2, one launch (start us, length us, event | category | flops | bytes accessed | tf_op | source)
XLA Modules:
  0.0 297.9 jit_solution(14104984194117521374)
XLA Ops:
  7.2 0.0 all-gather.6.cloned.1.call-start
  7.2 0.8 negate_multiply_fusion
  8.0 0.1 copy.40
  8.1 0.2 reduce_window_sum.22
  8.4 1.0 copy.43
  9.4 0.3 convolution_convert_fusion.2
  9.7 0.2 scatter.9
  9.9 0.7 pad_maximum_fusion
  10.5 0.0 all-gather.6.cloned.1.call-update
  10.6 0.0 all-gather.4.cloned.1.call-start
  10.7 0.1 copy.44
  10.7 1.0 convert_multiply_fusion.1
  11.8 0.1 copy.48
  11.9 0.7 fusion.46
  12.6 0.3 reduce_window_sum.23
  12.9 0.9 fusion.55
  13.8 50.6 %all-gather.6.cloned.1.call-done = bf16[16640,128]{1,0:T(8,128)(2,1)} async-done(((bf16[520,128]{1,0:T(8,128)(2,1)}), bf16[16640,128]{1,0:T(8,128)(2,1)}) %all-gather.6.cloned.1.call-update) | async-done | bytes 4259856 | tf_op jit(solution)/shard_map/all_gather | solution.py:49
  64.4 0.9 fusion.53
  65.4 0.1 copy.52
  65.5 0.1 copy.53
  65.6 0.1 select_reduce_fusion
  65.7 0.1 exponential_select_fusion
  65.8 0.1 mul.89
  65.9 0.1 mul.90
  66.0 4.4 %multiply_reduce_fusion = f32[512,128]{1,0:T(8,128)S(1)} fusion(bf16[32,520,128]{2,1,0:T(8,128)(2,1)} %bitcast.55, f32[32,512]{1,0:T(8,128)S(1)} %mul.90), kind=kLoop, calls=%fused_computation | loop fusion | flops 6225920 | bytes 4521984 | tf_op jit(solution)/shard_map/reduce_sum | solution.py:62
  70.4 0.3 fusion.14
  70.7 0.8 multiply_reduce_fusion.1
  71.5 0.1 copy.49
  71.7 0.2 convolution_convert_fusion.1
  72.0 21.9 %all_to_all.10 = bf16[8,48,512]{2,1,0:T(8,128)(2,1)S(1)} all-to-all(bf16[8,48,512]{2,1,0:T(8,128)(2,1)S(1)} %convolution_convert_fusion.1), channel_id=1, replica_groups=mesh['chip'=16,'core'=2,'exp'=8] {'exp'}, dimensions={0} | all-to-all | bytes 786432 | tf_op jit(solution)/shard_map/all_to_all | solution.py:110
  93.9 0.1 convert_bitcast_fusion
  94.0 0.1 copy.55
  94.0 0.2 fusion.16
  94.2 0.9 multiply_convert_fusion.2
  95.2 0.0 reduce-scatter.2.cloned.1.call-start
  95.2 0.1 collective-permute-start
  95.3 0.5 collective-permute-start.1
  95.8 0.1 collective-permute-start.2
  95.9 5.4 %collective-permute-done = bf16[4096,384]{1,0:T(8,128)(2,1)} collective-permute-done((bf16[4096,384]{1,0:T(8,128)(2,1)}, bf16[4096,384]{1,0:T(8,128)(2,1)}, u32[]{:S(2)}, u32[]{:S(2)}) %collective-permute-start) | collective-permute-done | bytes 3145760 | tf_op jit(solution)/shard_map/ppermute | solution.py:122
  101.3 54.9 %all-gather.4.cloned.1.call-done = bf16[768,4096]{1,0:T(8,128)(2,1)} async-done(((bf16[48,4096]{1,0:T(8,128)(2,1)}), bf16[768,4096]{1,0:T(8,128)(2,1)}) %all-gather.4.cloned.1.call-update) | async-done | bytes 6291472 | tf_op jit(solution)/shard_map/all_gather | solution.py:125
  156.2 9.8 %fusion = f32[768,768]{1,0:T(8,128)S(1)} fusion(bf16[768,4096]{1,0:T(8,128)(2,1)} %all-gather.4.cloned.1.call-done, bf16[4096,384]{1,0:T(8,128)(2,1)} %collective-permute-done, bf16[4096,384]{1,0:T(8,128)(2,1)} %bitcast.65), kind=kOutput, calls=%fused_computation.2 | convolution fusion | flops 4844421120 | bytes 14942208 | tf_op jit(solution)/shard_map/dot_general | solution.py:129
  166.0 7.1 %fusion.4 = f32[768,768]{1,0:T(8,128)S(1)} fusion(bf16[768,4096]{1,0:T(8,128)(2,1)S(1)} %copy-done.8, bf16[4096,384]{1,0:T(8,128)(2,1)} %collective-permute-done.1, bf16[4096,384]{1,0:T(8,128)(2,1)S(1)} %bitcast.67), kind=kOutput, calls=%fused_computation.6 | convolution fusion | flops 4844421120 | bytes 14942208 | tf_op jit(solution)/shard_map/dot_general | solution.py:130
  173.1 8.9 %convolution_convert_fusion = bf16[768,4096]{1,0:T(8,128)(2,1)} fusion(bf16[384,4096]{1,0:T(8,128)(2,1)} %collective-permute-done.2, bf16[384,4096]{1,0:T(8,128)(2,1)S(1)} %bitcast.69, f32[768,768]{1,0:T(8,128)S(1)} %fusion.4, f32[768,768]{1,0:T(8,128)S(1)} %fusion), kind=kOutput, calls=%fused_computation.1 | convolution fusion | flops 4851105792 | bytes 17301504 | tf_op jit(solution)/shard_map/dot_general | solution.py:132
  182.0 86.4 %reduce-scatter.2.cloned.1.call-done = bf16[48,4096]{1,0:T(8,128)(2,1)} async-done(((bf16[768,4096]{1,0:T(8,128)(2,1)}), bf16[48,4096]{1,0:T(8,128)(2,1)}) %reduce-scatter.2.cloned.1.call-update) | async-done | bytes 393232 | tf_op jit(solution)/shard_map/reduce_scatter | solution.py:133
  268.4 1.8 copy.57
  270.2 7.0 %all-to-all-start.1 = ((bf16[8,48,512]{2,1,0:T(8,128)(2,1)}), bf16[8,48,512]{2,1,0:T(8,128)(2,1)S(1)}, u32[]{:S(2)}, u32[]{:S(2)}) async-start(bf16[8,48,512]{2,1,0:T(8,128)(2,1)} %bitcast.53), calls=%async_computation.2 | async-start | bytes 786432 | tf_op jit(solution)/shard_map/all_to_all | solution.py:135
  277.2 13.1 %all-to-all-done.1 = bf16[8,48,512]{2,1,0:T(8,128)(2,1)S(1)} async-done(((bf16[8,48,512]{2,1,0:T(8,128)(2,1)}), bf16[8,48,512]{2,1,0:T(8,128)(2,1)S(1)}, u32[]{:S(2)}, u32[]{:S(2)}) %all-to-all-start.1) | async-done | bytes 393248 | tf_op jit(solution)/shard_map/all_to_all | solution.py:135
  290.3 1.1 fusion.15
  (43 shorter events, 0.4 us)
Async XLA Ops:
  7.2 2.3 copy-start
  7.2 63.2 %copy-start.2 = (bf16[128,128]{1,0:T(8,128)(2,1)S(1)}, bf16[128,128]{1,0:T(8,128)(2,1)}, u32[]{:S(2)}) copy-start(bf16[128,128]{1,0:T(8,128)(2,1)} %param.21) | copy-start | bytes 98308
  7.2 57.3 %all-gather.6.cloned.1.call-start = ((), (), s32[]{:S(2)}) async-start(), calls=%async_computation.5 | async-start | bytes 4392960 | tf_op jit(solution)/shard_map/all_gather | solution.py:49
  10.6 145.6 %all-gather.4.cloned.1.call-start = ((), (), s32[]{:S(2)}) async-start(), calls=%async_computation.3 | async-start | bytes 6684672 | tf_op jit(solution)/shard_map/all_gather | solution.py:125
  11.7 59.9 %copy-start.3 = (bf16[128,512]{1,0:T(8,128)(2,1)S(1)}, bf16[128,512]{1,0:T(8,128)(2,1)}, u32[]{:S(2)}) copy-start(bf16[128,512]{1,0:T(8,128)(2,1)} %param.25) | copy-start | bytes 393220
  11.7 59.9 %copy-start.6 = (f32[512]{0:T(512)S(1)}, f32[512]{0:T(512)}, u32[]{:S(2)}) copy-start(f32[512]{0:T(512)} %param.24) | copy-start | bytes 6148
  70.4 23.9 %copy-start.4 = (f32[4096]{0:T(1024)S(1)}, f32[4096]{0:T(1024)}, u32[]{:S(2)}) copy-start(f32[4096]{0:T(1024)} %param.26) | copy-start | bytes 49156
  71.7 94.2 %copy-start.1 = (bf16[128,512]{1,0:T(8,128)(2,1)}, bf16[128,512]{1,0:T(8,128)(2,1)S(1)}, u32[]{:S(2)}) copy-start(bf16[128,512]{1,0:T(8,128)(2,1)S(1)} %add_convert_fusion) | copy-start | bytes 393220
  95.2 173.2 %reduce-scatter.2.cloned.1.call-start = ((), (), s32[]{:S(2)}) async-start(), calls=%async_computation.4 | async-start | bytes 6684672 | tf_op jit(solution)/shard_map/reduce_scatter | solution.py:133
  95.2 6.1 %collective-permute-start = (bf16[4096,384]{1,0:T(8,128)(2,1)}, bf16[4096,384]{1,0:T(8,128)(2,1)}, u32[]{:S(2)}, u32[]{:S(2)}) collective-permute-start(bf16[4096,384]{1,0:T(8,128)(2,1)} %bitcast.64), channel_id=1, source_target_pairs={{0,8},{8,0},{1,9},{9,1},{2,10},{10,2},{3,11},{11,3},{4,12},{12,4},... | collective-permute-start | bytes 9437192 | tf_op jit(solution)/shard_map/ppermute | solution.py:122
  95.3 70.7 %collective-permute-start.1 = (bf16[4096,384]{1,0:T(8,128)(2,1)}, bf16[4096,384]{1,0:T(8,128)(2,1)}, u32[]{:S(2)}, u32[]{:S(2)}) collective-permute-start(bf16[4096,384]{1,0:T(8,128)(2,1)} %bitcast.66), channel_id=1, source_target_pairs={{0,8},{8,0},{1,9},{9,1},{2,10},{10,2},{3,11},{11,3},{4,12},{12,4},... | collective-permute-start | bytes 9437192 | tf_op jit(solution)/shard_map/ppermute | solution.py:123
  95.8 70.2 %copy-start.9 = (bf16[1,4096,384]{2,1,0:T(8,128)(2,1)S(1)}, bf16[1,4096,384]{2,1,0:T(8,128)(2,1)}, u32[]{:S(2)}) copy-start(bf16[1,4096,384]{2,1,0:T(8,128)(2,1)} %param.28) | copy-start | bytes 9437188
  95.8 77.3 %collective-permute-start.2 = (bf16[384,4096]{1,0:T(8,128)(2,1)}, bf16[384,4096]{1,0:T(8,128)(2,1)}, u32[]{:S(2)}, u32[]{:S(2)}) collective-permute-start(bf16[384,4096]{1,0:T(8,128)(2,1)} %bitcast.68), channel_id=1, source_target_pairs={{0,8},{8,0},{1,9},{9,1},{2,10},{10,2},{3,11},{11,3},{4,12},{12,4},... | collective-permute-start | bytes 9437192 | tf_op jit(solution)/shard_map/ppermute | solution.py:124
  156.2 9.8 %copy-start.8 = (bf16[768,4096]{1,0:T(8,128)(2,1)S(1)}, bf16[768,4096]{1,0:T(8,128)(2,1)}, u32[]{:S(2)}) copy-start(bf16[768,4096]{1,0:T(8,128)(2,1)} %all-gather.4.cloned.1.call-done) | copy-start | bytes 18874372
  166.0 7.2 %copy-start.10 = (bf16[1,384,4096]{2,1,0:T(8,128)(2,1)S(1)}, bf16[1,384,4096]{2,1,0:T(8,128)(2,1)}, u32[]{:S(2)}) copy-start(bf16[1,384,4096]{2,1,0:T(8,128)(2,1)} %param.29) | copy-start | bytes 9437188
  182.0 95.2 %copy-start.5 = (s32[128,2]{0,1:T(2,128)S(1)}, s32[128,2]{0,1:T(2,128)}, u32[]{:S(2)}) copy-start(s32[128,2]{0,1:T(2,128)} %param.30) | copy-start | bytes 3076
  182.0 95.2 %copy-start.7 = (f32[128,2]{0,1:T(2,128)S(1)}, f32[128,2]{0,1:T(2,128)}, u32[]{:S(2)}) copy-start(f32[128,2]{0,1:T(2,128)} %param.31) | copy-start | bytes 3076
  270.2 20.1 %all-to-all-start.1 = ((bf16[8,48,512]{2,1,0:T(8,128)(2,1)}), bf16[8,48,512]{2,1,0:T(8,128)(2,1)S(1)}, u32[]{:S(2)}, u32[]{:S(2)}) async-start(bf16[8,48,512]{2,1,0:T(8,128)(2,1)} %bitcast.53), calls=%async_computation.2 | async-start | bytes 786432 | tf_op jit(solution)/shard_map/all_to_all | solution.py:135
Sparse Core Ops, SparseCore 0:
  10.7 53.7 all-gather.5
  95.3 60.8 all-gather.3
  182.2 86.1 reduce-scatter.1
where the time goes:
time: 298 us
  waiting for transfers between devices  210 us (70%)
  matrix products  29.3 us (10%)
  blocking collectives  21.9 us (7%)
  between operations  14.1 us (5%)
  other arithmetic  9.51 us (3%)
  starting transfers between devices  7.8 us (3%)
  local copies, waits for them, and re-layouts  4.92 us (2%)
    reduce_scatter x1, waiting for transfers between devices, on_device(): summed = lax.psum_scatter(pair_sum, 'chip', scatter_dimension=0, tiled=True)  86.4 us
    all_gather x1, waiting for transfers between devices, on_device(): token_piece = lax.all_gather(chosen, 'chip', axis=0, tiled=True)  54.9 us
    all_gather x1, waiting for transfers between devices, carried_state(): everything = lax.all_gather(packed, CTX)  50.6 us
    all_to_all x1, blocking collectives, on_device(): arrived = lax.all_to_all(picked, 'exp', 0, 0)  21.9 us
    all_to_all x1, waiting for transfers between devices, on_device(): returned = lax.all_to_all(outgoing, 'exp', 0, 0)  13.1 us
    dot_general x1, matrix products, on_device(): jnp.dot(token_piece, gate_both, preferred_element_type=jnp.float32)  9.77 us
    dot_general x1, matrix products, on_device(): jnp.dot(hidden, down_both, preferred_element_type=jnp.float32)  8.86 us
    dot_general x1, matrix products, on_device(): up_proj = jnp.dot(token_piece, up_both, preferred_element_type=jnp.float32)  7.1 us
  transfers between devices with their start and end apart: 7, of which 5 were waited for; matrix products, arithmetic and copies ran while one was open for 7% of the time, Pallas kernels for 0%

commit v1 on v0

--- a/solution.py
+++ b/solution.py
@@ -122,7 +122,9 @@
     gate_other = lax.ppermute(gate_here, "core", swap)
     up_other = lax.ppermute(up_here, "core", swap)
     down_other = lax.ppermute(down_here, "core", swap)
-    token_piece = lax.all_gather(chosen, "chip", axis=0, tiled=True)
+    token_piece = jnp.concatenate(
+        lax.all_to_all(jnp.stack([chosen] * lax.axis_size("chip")), "chip", 0, 0), axis=0
+    )
     gate_both = jnp.concatenate([gate_here, gate_other], axis=1)
     up_both = jnp.concatenate([up_here, up_other], axis=1)
     down_both = jnp.concatenate([down_here, down_other], axis=0)

time: 298 us -> 335 us (1.12)
  waiting for transfers between devices: 210 us -> 237 us
  starting transfers between devices: 7.8 us -> 13.8 us
  local copies, waits for them, and re-layouts: 4.92 us -> 8.36 us
    all_to_all x0 -> x1, waiting for transfers between devices: none -> 82.5 us  [on_device(): lax.all_to_all(jnp.stack([chosen] * lax.axis_size('chip')), 'chip', 0, 0)]
    all_gather x1 -> x0, waiting for transfers between devices: 54.9 us -> none  [on_device(): token_piece = lax.all_gather(chosen, 'chip', axis=0, tiled=True)]
    all_to_all x0 -> x1, starting transfers between devices: none -> 6.01 us  [on_device(): lax.all_to_all(jnp.stack([chosen] * lax.axis_size('chip')), 'chip', 0, 0)]
    another operation x0 -> x1, local copies, waits for them, and re-layouts: none -> 3.44 us  [on_device(): jnp.stack([chosen] * lax.axis_size('chip'))]
  transfers between devices with their start and end apart: 7 -> 7, of which waited for: 5 -> 5; matrix products, arithmetic and copies ran while one was open for 7% -> 6% of each run, Pallas kernels for 0% -> 0%
where the time goes in v1:
time: 335 us; the launch traced here: 334 us
  waiting for transfers between devices  237 us (71%)
  matrix products  30.3 us (9%)
  blocking collectives  21.9 us (7%)
  between operations  14.4 us (4%)
  starting transfers between devices  13.8 us (4%)
  other arithmetic  8.76 us (3%)
  local copies, waits for them, and re-layouts  8.36 us (2%)
    reduce_scatter x1, waiting for transfers between devices, on_device(): summed = lax.psum_scatter(pair_sum, 'chip', scatter_dimension=0, tiled=True)  85.2 us
    all_to_all x1, waiting for transfers between devices, on_device(): lax.all_to_all(jnp.stack([chosen] * lax.axis_size('chip')), 'chip', 0, 0)  82.5 us
    all_gather x1, waiting for transfers between devices, carried_state(): everything = lax.all_gather(packed, CTX)  50.7 us
    all_to_all x1, blocking collectives, on_device(): arrived = lax.all_to_all(picked, 'exp', 0, 0)  21.9 us
    all_to_all x1, waiting for transfers between devices, on_device(): returned = lax.all_to_all(outgoing, 'exp', 0, 0)  13 us
    dot_general x1, matrix products, on_device(): jnp.dot(hidden, down_both, preferred_element_type=jnp.float32)  8.94 us
    dot_general x1, matrix products, on_device(): up_proj = jnp.dot(token_piece, up_both, preferred_element_type=jnp.float32)  8.92 us
    dot_general x1, matrix products, on_device(): jnp.dot(token_piece, gate_both, preferred_element_type=jnp.float32)  8.92 us
  transfers between devices with their start and end apart: 7, of which 5 were waited for; matrix products, arithmetic and copies ran while one was open for 6% of the time, Pallas kernels for 0%

profile of v1, /device:TPU:2, one launch (start us, length us, event | category | flops | bytes accessed | tf_op | source)
XLA Modules:
  0.0 334.2 jit_solution(14264616988498677255)
XLA Ops:
  7.2 0.0 all-gather.3.cloned.1.call-start
  7.2 0.8 negate_multiply_fusion
  8.0 0.1 copy.40
  8.1 0.2 reduce_window_sum.22
  8.4 1.0 copy.43
  9.4 0.3 convolution_convert_fusion.2
  9.7 0.2 scatter.9
  9.9 0.7 pad_maximum_fusion
  10.6 0.1 copy.44
  10.7 1.0 convert_multiply_fusion.1
  11.7 0.1 copy.48
  11.8 0.7 fusion.46
  12.5 0.3 reduce_window_sum.23
  12.9 0.9 fusion.55
  13.8 50.7 %all-gather.3.cloned.1.call-done = bf16[16640,128]{1,0:T(8,128)(2,1)} async-done(((bf16[520,128]{1,0:T(8,128)(2,1)}), bf16[16640,128]{1,0:T(8,128)(2,1)}) %all-gather.3.cloned.1.call-update) | async-done | bytes 4259856 | tf_op jit(solution)/shard_map/all_gather | solution.py:49
  64.4 0.9 fusion.53
  65.4 0.1 copy.52
  65.5 0.1 copy.53
  65.6 0.1 select_reduce_fusion
  65.7 0.1 exponential_select_fusion
  65.8 0.1 mul.93
  65.9 0.1 mul.94
  66.0 4.4 %multiply_reduce_fusion = f32[512,128]{1,0:T(8,128)S(1)} fusion(bf16[32,520,128]{2,1,0:T(8,128)(2,1)} %bitcast.56, f32[32,512]{1,0:T(8,128)S(1)} %mul.94), kind=kLoop, calls=%fused_computation | loop fusion | flops 6225920 | bytes 4521984 | tf_op jit(solution)/shard_map/reduce_sum | solution.py:62
  70.4 0.3 fusion.14
  70.7 0.8 multiply_reduce_fusion.1
  71.5 0.1 copy.49
  71.7 0.2 convolution_convert_fusion.1
  72.0 21.9 %all_to_all.15 = bf16[8,48,512]{2,1,0:T(8,128)(2,1)S(1)} all-to-all(bf16[8,48,512]{2,1,0:T(8,128)(2,1)S(1)} %convolution_convert_fusion.1), channel_id=1, replica_groups=mesh['chip'=16,'core'=2,'exp'=8] {'exp'}, dimensions={0} | all-to-all | bytes 786432 | tf_op jit(solution)/shard_map/all_to_all | solution.py:110
  93.9 0.1 convert_bitcast_fusion
  94.0 0.1 copy.55
  94.0 0.2 fusion.16
  94.2 0.1 multiply_convert_fusion.2
  94.4 3.4 %stack.2 = bf16[16,48,4096]{2,1,0:T(8,128)(2,1)} broadcast(bf16[48,4096]{1,0:T(8,128)(2,1)S(1)} %multiply_convert_fusion.2), dimensions={1,2} | broadcast | bytes 6684672 | tf_op jit(solution)/shard_map/stack | solution.py:126
  97.8 6.0 %all-to-all-start.1 = ((bf16[16,48,4096]{2,1,0:T(8,128)(2,1)}), bf16[16,48,4096]{2,1,0:T(8,128)(2,1)}, u32[]{:S(2)}, u32[]{:S(2)}) async-start(bf16[16,48,4096]{2,1,0:T(8,128)(2,1)} %stack.2), calls=%async_computation.1 | async-start | bytes 12582912 | tf_op jit(solution)/shard_map/all_to_all | solution.py:126
  103.8 0.0 reduce-scatter.2.cloned.1.call-start
  103.9 0.1 collective-permute-start
  104.0 0.5 collective-permute-start.1
  104.5 0.1 collective-permute-start.2
  104.6 5.2 %collective-permute-done = bf16[4096,384]{1,0:T(8,128)(2,1)} collective-permute-done((bf16[4096,384]{1,0:T(8,128)(2,1)S(1)}, bf16[4096,384]{1,0:T(8,128)(2,1)}, u32[]{:S(2)}, u32[]{:S(2)}) %collective-permute-start) | collective-permute-done | bytes 3145760 | tf_op jit(solution)/shard_map/ppermute | solution.py:122
  109.8 82.5 %all-to-all-done.1 = bf16[16,48,4096]{2,1,0:T(8,128)(2,1)} async-done(((bf16[16,48,4096]{2,1,0:T(8,128)(2,1)}), bf16[16,48,4096]{2,1,0:T(8,128)(2,1)}, u32[]{:S(2)}, u32[]{:S(2)}) %all-to-all-start.1) | async-done | bytes 6291488 | tf_op jit(solution)/shard_map/all_to_all | solution.py:126
  192.3 8.9 %fusion = f32[768,768]{1,0:T(8,128)S(1)} fusion(bf16[768,4096]{1,0:T(8,128)(2,1)} %bitcast.14, bf16[4096,384]{1,0:T(8,128)(2,1)} %collective-permute-done, bf16[4096,384]{1,0:T(8,128)(2,1)S(1)} %bitcast.66), kind=kOutput, calls=%fused_computation.2 | convolution fusion | flops 4844421120 | bytes 14942208 | tf_op jit(solution)/shard_map/dot_general | solution.py:131
  201.2 8.9 %fusion.4 = f32[768,768]{1,0:T(8,128)S(1)} fusion(bf16[768,4096]{1,0:T(8,128)(2,1)} %bitcast.14, bf16[4096,384]{1,0:T(8,128)(2,1)} %collective-permute-done.1, bf16[4096,384]{1,0:T(8,128)(2,1)S(1)} %bitcast.68), kind=kOutput, calls=%fused_computation.6 | convolution fusion | flops 4844421120 | bytes 14942208 | tf_op jit(solution)/shard_map/dot_general | solution.py:132
  210.2 8.9 %convolution_convert_fusion = bf16[768,4096]{1,0:T(8,128)(2,1)} fusion(bf16[384,4096]{1,0:T(8,128)(2,1)} %collective-permute-done.2, bf16[384,4096]{1,0:T(8,128)(2,1)S(1)} %bitcast.70, f32[768,768]{1,0:T(8,128)S(1)} %fusion.4, f32[768,768]{1,0:T(8,128)S(1)} %fusion), kind=kOutput, calls=%fused_computation.1 | convolution fusion | flops 4851105792 | bytes 17301504 | tf_op jit(solution)/shard_map/dot_general | solution.py:134
  219.2 85.2 %reduce-scatter.2.cloned.1.call-done = bf16[48,4096]{1,0:T(8,128)(2,1)} async-done(((bf16[768,4096]{1,0:T(8,128)(2,1)}), bf16[48,4096]{1,0:T(8,128)(2,1)}) %reduce-scatter.2.cloned.1.call-update) | async-done | bytes 393232 | tf_op jit(solution)/shard_map/reduce_scatter | solution.py:135
  304.4 1.8 copy.57
  306.2 7.0 %all-to-all-start.2 = ((bf16[8,48,512]{2,1,0:T(8,128)(2,1)}), bf16[8,48,512]{2,1,0:T(8,128)(2,1)S(1)}, u32[]{:S(2)}, u32[]{:S(2)}) async-start(bf16[8,48,512]{2,1,0:T(8,128)(2,1)} %bitcast.54), calls=%async_computation.3 | async-start | bytes 786432 | tf_op jit(solution)/shard_map/all_to_all | solution.py:137
  313.2 13.0 %all-to-all-done.2 = bf16[8,48,512]{2,1,0:T(8,128)(2,1)S(1)} async-done(((bf16[8,48,512]{2,1,0:T(8,128)(2,1)}), bf16[8,48,512]{2,1,0:T(8,128)(2,1)S(1)}, u32[]{:S(2)}, u32[]{:S(2)}) %all-to-all-start.2) | async-done | bytes 393248 | tf_op jit(solution)/shard_map/all_to_all | solution.py:137
  326.3 1.1 fusion.15
  (43 shorter events, 0.4 us)
Async XLA Ops:
  7.2 2.3 copy-start
  7.2 63.2 %copy-start.2 = (bf16[128,128]{1,0:T(8,128)(2,1)S(1)}, bf16[128,128]{1,0:T(8,128)(2,1)}, u32[]{:S(2)}) copy-start(bf16[128,128]{1,0:T(8,128)(2,1)} %param.21) | copy-start | bytes 98308
  7.2 57.3 %all-gather.3.cloned.1.call-start = ((), (), s32[]{:S(2)}) async-start(), calls=%async_computation.5 | async-start | bytes 4392960 | tf_op jit(solution)/shard_map/all_gather | solution.py:49
  11.7 60.0 %copy-start.3 = (bf16[128,512]{1,0:T(8,128)(2,1)S(1)}, bf16[128,512]{1,0:T(8,128)(2,1)}, u32[]{:S(2)}) copy-start(bf16[128,512]{1,0:T(8,128)(2,1)} %param.25) | copy-start | bytes 393220
  11.7 60.0 %copy-start.6 = (f32[512]{0:T(512)S(1)}, f32[512]{0:T(512)}, u32[]{:S(2)}) copy-start(f32[512]{0:T(512)} %param.24) | copy-start | bytes 6148
  70.4 23.9 %copy-start.4 = (f32[4096]{0:T(1024)S(1)}, f32[4096]{0:T(1024)}, u32[]{:S(2)}) copy-start(f32[4096]{0:T(1024)} %param.26) | copy-start | bytes 49156
  71.7 26.1 %copy-start.1 = (bf16[128,512]{1,0:T(8,128)(2,1)}, bf16[128,512]{1,0:T(8,128)(2,1)S(1)}, u32[]{:S(2)}) copy-start(bf16[128,512]{1,0:T(8,128)(2,1)S(1)} %add_convert_fusion) | copy-start | bytes 393220
  97.8 6.1 %copy-start.8 = (bf16[1,4096,384]{2,1,0:T(8,128)(2,1)S(1)}, bf16[1,4096,384]{2,1,0:T(8,128)(2,1)}, u32[]{:S(2)}) copy-start(bf16[1,4096,384]{2,1,0:T(8,128)(2,1)} %param.27) | copy-start | bytes 9437188
  97.8 94.5 %all-to-all-start.1 = ((bf16[16,48,4096]{2,1,0:T(8,128)(2,1)}), bf16[16,48,4096]{2,1,0:T(8,128)(2,1)}, u32[]{:S(2)}, u32[]{:S(2)}) async-start(bf16[16,48,4096]{2,1,0:T(8,128)(2,1)} %stack.2), calls=%async_computation.1 | async-start | bytes 12582912 | tf_op jit(solution)/shard_map/all_to_all | solution.py:126
  103.8 200.5 %reduce-scatter.2.cloned.1.call-start = ((), (), s32[]{:S(2)}) async-start(), calls=%async_computation.4 | async-start | bytes 6684672 | tf_op jit(solution)/shard_map/reduce_scatter | solution.py:135
  103.9 5.9 %collective-permute-start = (bf16[4096,384]{1,0:T(8,128)(2,1)S(1)}, bf16[4096,384]{1,0:T(8,128)(2,1)}, u32[]{:S(2)}, u32[]{:S(2)}) collective-permute-start(bf16[4096,384]{1,0:T(8,128)(2,1)S(1)} %bitcast.65), channel_id=1, source_target_pairs={{0,8},{8,0},{1,9},{9,1},{2,10},{10,2},{3,11},{11,3},{4,12},{12,4},... | collective-permute-start | bytes 9437192 | tf_op jit(solution)/shard_map/ppermute | solution.py:122
  104.0 97.2 %collective-permute-start.1 = (bf16[4096,384]{1,0:T(8,128)(2,1)}, bf16[4096,384]{1,0:T(8,128)(2,1)}, u32[]{:S(2)}, u32[]{:S(2)}) collective-permute-start(bf16[4096,384]{1,0:T(8,128)(2,1)} %bitcast.67), channel_id=1, source_target_pairs={{0,8},{8,0},{1,9},{9,1},{2,10},{10,2},{3,11},{11,3},{4,12},{12,4},... | collective-permute-start | bytes 9437192 | tf_op jit(solution)/shard_map/ppermute | solution.py:123
  104.5 105.7 %collective-permute-start.2 = (bf16[384,4096]{1,0:T(8,128)(2,1)}, bf16[384,4096]{1,0:T(8,128)(2,1)}, u32[]{:S(2)}, u32[]{:S(2)}) collective-permute-start(bf16[384,4096]{1,0:T(8,128)(2,1)} %bitcast.69), channel_id=1, source_target_pairs={{0,8},{8,0},{1,9},{9,1},{2,10},{10,2},{3,11},{11,3},{4,12},{12,4},... | collective-permute-start | bytes 9437192 | tf_op jit(solution)/shard_map/ppermute | solution.py:124
  192.3 9.0 %copy-start.9 = (bf16[1,4096,384]{2,1,0:T(8,128)(2,1)S(1)}, bf16[1,4096,384]{2,1,0:T(8,128)(2,1)}, u32[]{:S(2)}) copy-start(bf16[1,4096,384]{2,1,0:T(8,128)(2,1)} %param.28) | copy-start | bytes 9437188
  201.2 9.0 %copy-start.10 = (bf16[1,384,4096]{2,1,0:T(8,128)(2,1)S(1)}, bf16[1,384,4096]{2,1,0:T(8,128)(2,1)}, u32[]{:S(2)}) copy-start(bf16[1,384,4096]{2,1,0:T(8,128)(2,1)} %param.29) | copy-start | bytes 9437188
  219.1 94.0 %copy-start.5 = (s32[128,2]{0,1:T(2,128)S(1)}, s32[128,2]{0,1:T(2,128)}, u32[]{:S(2)}) copy-start(s32[128,2]{0,1:T(2,128)} %param.30) | copy-start | bytes 3076
  219.1 94.0 %copy-start.7 = (f32[128,2]{0,1:T(2,128)S(1)}, f32[128,2]{0,1:T(2,128)}, u32[]{:S(2)}) copy-start(f32[128,2]{0,1:T(2,128)} %param.31) | copy-start | bytes 3076
  306.2 20.1 %all-to-all-start.2 = ((bf16[8,48,512]{2,1,0:T(8,128)(2,1)}), bf16[8,48,512]{2,1,0:T(8,128)(2,1)S(1)}, u32[]{:S(2)}, u32[]{:S(2)}) async-start(bf16[8,48,512]{2,1,0:T(8,128)(2,1)} %bitcast.54), calls=%async_computation.3 | async-start | bytes 786432 | tf_op jit(solution)/shard_map/all_to_all | solution.py:137
Sparse Core Ops, SparseCore 0:
  10.7 53.7 all-gather.2
  219.3 85.0 reduce-scatter.1
